TPU v7x, 32 devices: a whole 2x2x4 slice. The times are simulated.
32 devices in a mesh: gx: 8 (over z, y), gy: 4 (over x, core).
Axes of the slice: x: 2, y: 2, z: 4, core: 2. Of those that a mesh axis runs over, the one named last changes fastest.
Arguments:
- queries: bfloat16 [8, 768, 2560], P('gx', 'gy'), may hold values from -7 to 7
- new_kv: bfloat16 [8, 768, 512], P('gx', 'gy'), may hold values from -7 to 7
- cache_pool: bfloat16 [8, 2048, 512], P('gx', 'gy'), may hold values from -6 to 6
- lengths: int32 [8], P('gx'), may hold values from 0 to 32768, as said below
- owner: int32 [8, 4], P('gx'), may hold values from 0 to 3, each once within a row
- w_out: bfloat16 [2560, 2560], P(None, ('gx', 'gy')), may hold values from -0.125 to 0.125
- last_residual: bfloat16 [8, 2560], P(None, ('gx', 'gy')), may hold values from -6 to 6
- norm_gain: bfloat16 [2560], replicated, may hold values from 0.5 to 1.5
- head: bfloat16 [256000, 2560], P(('gx', 'gy')), may hold values from -11 to 11
- targets: int32 [8], replicated, may hold values from 0 to 255999
Outputs:
- mixed_out: bfloat16 [8, 768, 2560], P('gx', 'gy')
- new_cache: bfloat16 [8, 2048, 512], P('gx', 'gy')
- log_norm: float32 [8], replicated
- top_logit: float32 [8], replicated
- target_logprob: float32 [8], replicated
Inputs may be any that keep to these rules, and one draw needn't show every extreme that they name: `lengths`: in every draw one request has seen 32768 tokens and one has seen none. `owner`: each row names every block index once.
All inputs are finite; a program needn't handle non-finite values.
Results may differ from a plain program's by a relative error of at most 0.0042.
Values may be sent and summed in bfloat16 or wider, within the bound.
No kernel may reach another device: no remote copies, remote signals or barrier semaphores. Data moves between devices by JAX's collectives and lax.ppermute only.
A program may use at most 128 MiB of HBM per device.

v0:
```python
import math
import jax
import jax.numpy as jnp
from jax import lax
from jax.sharding import PartitionSpec as P


def on_device(
    queries, new_kv, cache_pool, lengths, owner, w_out, last_residual, norm_gain, head, targets
):
    req_local, new_local, model_cols = queries.shape
    slot_count = cache_pool.shape[1]
    entry_width = new_kv.shape[2]
    head_dim = entry_width // 2
    head_count = model_cols // head_dim
    group_pos = lax.axis_size("gy")
    my_index = lax.axis_index("gy")
    new_total = new_local * group_pos
    window_len = slot_count * group_pos
    keep_len = window_len - new_total
    score_scale = 1.0 / math.sqrt(head_dim)
    query_heads = queries.reshape(req_local, new_local, head_count, head_dim)
    query_pos = my_index * new_local + jnp.arange(new_local, dtype=jnp.int32)
    first_slot = window_len - lengths
    block_ids = jnp.arange(group_pos, dtype=jnp.int32)
    matches = owner[:, :, None] == block_ids[None, None, :]
    logical = jnp.sum(jnp.where(matches, block_ids[None, :, None], 0), axis=1)
    own_block = lax.dynamic_index_in_dim(logical, my_index, axis=1, keepdims=False)
    slot_ids = jnp.arange(slot_count, dtype=jnp.int32)
    new_ids = jnp.arange(new_local, dtype=jnp.int32)
    target_slot = own_block[:, None] * slot_count + slot_ids[None, :]
    from_old = target_slot < keep_len
    old_slot = jnp.minimum(target_slot + new_total, window_len - 1)
    old_block = jnp.take_along_axis(owner, old_slot // slot_count, axis=1)
    pool_row = old_block * slot_count + old_slot % slot_count
    new_row = jnp.maximum(target_slot - keep_len, 0)
    source_cache = jnp.where(from_old, pool_row, -1)
    source_new = jnp.where(from_old, -1, new_row)

    def cache_keys(shard_ids):
        chosen = jnp.take(logical, shard_ids, axis=1)
        slot_pos = (chosen[:, :, None] * slot_count + slot_ids[None, None, :]).reshape(
            req_local, -1
        )
        return (slot_pos[:, None, :] >= query_pos[None, :, None]) & (
            slot_pos[:, None, :] >= first_slot[:, None, None]
        )

    def new_keys(shard_ids):
        positions = (shard_ids[:, None] * new_local + new_ids[None, :]).reshape(-1)
        seen_new = positions[None, :] <= query_pos[:, None]
        return seen_new[None]

    def attend(carried, key_rows, visible):
        running_max, weight_sum, accumulated = carried
        scores = (
            jnp.einsum(
                "rthd,rnd->rthn",
                query_heads,
                key_rows[:, :, :head_dim],
                preferred_element_type=jnp.float32,
            )
            * score_scale
        )
        allowed = visible[:, :, None, :]
        block_max = jnp.max(jnp.where(allowed, scores, -1e30), axis=3)
        new_max = jnp.maximum(running_max, block_max)
        weights = jnp.where(allowed, jnp.exp(scores - new_max[..., None]), 0.0)
        rescale = jnp.exp(running_max - new_max)
        weight_sum = rescale * weight_sum + jnp.sum(weights, axis=3)
        accumulated = rescale[..., None] * accumulated + jnp.einsum(
            "rthn,rnd->rthd",
            weights.astype(jnp.bfloat16),
            key_rows[:, :, head_dim:],
            preferred_element_type=jnp.float32,
        )
        return (new_max, weight_sum, accumulated)

    def copy_rows(fresh_block, part_rows, source, base_row):
        local_row = source - base_row
        inside = (local_row >= 0) & (local_row < part_rows.shape[1])
        clipped = jnp.clip(local_row, 0, part_rows.shape[1] - 1)
        picked = jnp.take_along_axis(part_rows, clipped[:, :, None], axis=1)
        return jnp.where(inside[:, :, None], picked, fresh_block)

    def make_step(shard_width, source, layout_kind, carried, shard_rows):
        shard_count = shard_rows.shape[1] // shard_width
        group_size = math.gcd(shard_count, 4)

        def turn_body(turn_index, inner_state):
            offset = turn_index * group_size * shard_width
            part_rows = lax.dynamic_slice_in_dim(shard_rows, offset, group_size * shard_width, 1)
            shard_ids = turn_index * group_size + jnp.arange(group_size, dtype=jnp.int32)
            if layout_kind == "cache":
                key_rows = part_rows
                visible = cache_keys(shard_ids)
            else:
                key_rows = part_rows
                visible = new_keys(shard_ids)
            softmax_state = lax.cond(
                jnp.any(visible),
                lambda state: attend(state, key_rows, visible),
                lambda state: state,
                inner_state[:3],
            )
            fresh_block = copy_rows(inner_state[3], part_rows, source, offset)
            return softmax_state + (fresh_block,)

        return lax.fori_loop(0, shard_count // group_size, turn_body, carried)

    initial = (
        jnp.full((req_local, new_local, head_count), -1e30, jnp.float32),
        jnp.zeros((req_local, new_local, head_count), jnp.float32),
        jnp.zeros((req_local, new_local, head_count, head_dim), jnp.float32),
        jnp.zeros((req_local, slot_count, entry_width), jnp.bfloat16),
    )
    carried = make_step(
        slot_count,
        source_cache,
        "cache",
        initial,
        lax.all_gather(cache_pool, "gy", axis=1, tiled=True),
    )
    carried = make_step(
        new_local, source_new, "new", carried, lax.all_gather(new_kv, "gy", axis=1, tiled=True)
    )
    running_max, weight_sum, accumulated, fresh_block = carried
    mixed_out = (
        (accumulated / weight_sum[..., None])
        .astype(jnp.bfloat16)
        .reshape(req_local, new_local, model_cols)
    )
    last_local = mixed_out[:, new_local - 1, :]
    group_req = lax.axis_size("gx")
    holder = (my_index == group_pos - 1).astype(jnp.float32)
    padded = jnp.zeros((req_local * group_req, model_cols), jnp.float32)
    padded = lax.dynamic_update_slice_in_dim(
        padded, last_local.astype(jnp.float32) * holder, lax.axis_index("gx") * req_local, 0
    )
    last_mixed = lax.psum(padded, ("gx", "gy")).astype(jnp.bfloat16)
    last_hidden = (
        last_residual.astype(jnp.float32)
        + jnp.dot(last_mixed, w_out, preferred_element_type=jnp.float32)
    ).astype(jnp.bfloat16)
    full_hidden = lax.all_gather(last_hidden, ("gx", "gy"), axis=1, tiled=True).astype(jnp.float32)
    normed = (
        full_hidden
        * lax.rsqrt(jnp.mean(full_hidden * full_hidden, axis=1, keepdims=True) + 1e-06)
        * norm_gain.astype(jnp.float32)
    ).astype(jnp.bfloat16)
    logits = lax.dot_general(
        normed, head, (((1,), (1,)), ((), ())), preferred_element_type=jnp.float32
    )
    vocab_local = head.shape[0]
    local_target = targets - lax.axis_index(("gx", "gy")) * vocab_local
    target_hit = jnp.arange(vocab_local, dtype=jnp.int32)[None, :] == local_target[:, None]
    picked = jnp.sum(jnp.where(target_hit, logits, 0.0), axis=1)
    local_top = jnp.max(logits, axis=1)
    top_logit = lax.pmax(local_top, ("gx", "gy"))
    exp_total, picked = lax.psum(
        (jnp.sum(jnp.exp(logits - top_logit[:, None]), axis=1), picked), ("gx", "gy")
    )
    log_norm = top_logit + jnp.log(exp_total)
    return (mixed_out, fresh_block, log_norm, top_logit, picked - log_norm)


def solution(mesh):
    placed = (
        P("gx", "gy", None),
        P("gx", "gy", None),
        P("gx", "gy", None),
        P("gx"),
        P("gx", None),
        P(None, ("gx", "gy")),
        P(None, ("gx", "gy")),
        P(),
        P(("gx", "gy"), None),
        P(),
    )
    return jax.shard_map(
        on_device,
        mesh=mesh,
        in_specs=placed,
        out_specs=(P("gx", "gy", None), P("gx", "gy", None), P(), P(), P()),
        check_vma=False,
    )
```

profile of v0, /device:TPU:0, one launch (start us, length us, event | category | flops | bytes accessed | tf_op | source)
XLA Modules:
  0.0 262.6 jit_solution(15581894182387955175)
XLA Ops:
  8.6 1.5 copy.34
  17.0 1.5 fusion.55
  18.4 2.6 compare_select_fusion
  21.1 14.6 %all_gather.10 = bf16[1,768,512]{2,1,0:T(8,128)(2,1)S(1)} all-gather(bf16[1,192,512]{2,1,0:T(8,128)(2,1)} %param.15), channel_id=1, replica_groups=mesh['gx'=8,'gy'=4] {'gy'}, dimensions={1}, use_global_device_ids=true | all-gather | bytes 983040 | tf_op jit(solution)/shard_map/all_gather | solution.py:125
  35.7 2.6 gather_fusion.1
  38.3 1.4 broadcast_in_dim.173
  40.3 2.6 compare_select_fusion.3
  44.7 15.8 %conditional.2 = ((f32[1,192,10]{1,2,0:T(8,128)S(1)}, f32[1,192,10]{1,2,0:T(8,128)S(1)}, f32[1,192,10,256]{3,1,2,0:T(8,128)})) conditional(s32[]{:T(128)} %convert_element_type.54, (f32[1,192,10]{1,2,0:T(8,128)S(1)}, f32[1,192,10]{1,2,0:T(8,128)S(1)}, f32[1,192,10,256]{3,1,2,0:T(8,128)}) %tuple.31, (pred[1,192,2048]{2,1,0:T(8,128)(4,1)S(1)}, ...), branch_computations={%region_3.4_spmd, %region_4.7_spmd} | conditional | flops 4070774272 | bytes 63906876 | solution.py:100
  44.7 5.7 %select_reduce_fusion = (f32[192,10]{0,1:T(8,128)S(1)}, f32[192,10,2048]{2,0,1:T(8,128)S(1)}) fusion(pred[192,2048]{1,0:T(8,128)(4,1)S(1)} %bitcast.103, bf16[1,2048,512]{2,1,0:T(8,128)(2,1)} %get-tuple-element.118, bf16[1,192,10,256]{1,3,2,0:T(8,128)(2,1)S(1)} %get-tuple-element.209), kind=kOutput, calls=%fused_computation.4 | convolution fusion | flops 2025060480 | bytes 18161152 | tf_op jit(solution)/shard_map/while/body/eval_jaxpr/cond/branch_1_fun/rthd,rnd->rthn/dot_general | solution.py:57
  50.4 5.4 %bitcast_add_fusion = f32[1,192,10,256]{3,1,2,0:T(8,128)} fusion(f32[1,192,10,256]{3,1,2,0:T(8,128)} %get-tuple-element.120, f32[192,10,2048]{2,0,1:T(8,128)S(1)} %get-tuple-element.243, f32[192,10]{0,1:T(8,128)S(1)} %bitcast.109, pred[192,2048]{1,0:T(8,128)(4,1)S(1)} %bitcast.104, bf16[1,2048,512]{2,1,0:T(8,128)(2,1)S(1)} %copy-done.2, ...), kind=kOutput, calls=%fused_computation.9 | convolution fusion | flops 2029977600 | bytes 21135360 | tf_op jit(solution)/shard_map/while/body/eval_jaxpr/cond/branch_1_fun/rthn,rnd->rthd/dot_general | solution.py:71
  55.8 4.7 %fusion.1 = f32[192,10]{0,1:T(8,128)S(1)} fusion(f32[192,10,2048]{2,0,1:T(8,128)S(1)} %get-tuple-element.243, f32[192,10]{0,1:T(8,128)S(1)} %bitcast.110, pred[192,2048]{1,0:T(8,128)(4,1)S(1)} %bitcast.105), kind=kLoop, calls=%fused_computation.6 | loop fusion | flops 15726720 | bytes 16137216 | tf_op jit(solution)/shard_map/while/body/eval_jaxpr/cond/branch_1_fun/reduce_sum | solution.py:70
  60.5 7.6 %conditional.3 = ((f32[1,192,10]{1,2,0:T(8,128)S(1)}, f32[1,192,10,256]{3,1,2,0:T(8,128)})) conditional(s32[]{:T(128)} %convert_element_type.53, (f32[1,192,10]{1,2,0:T(8,128)S(1)}, f32[1,192,10,256]{3,1,2,0:T(8,128)}) %tuple.33, (s32[768]{0:T(1024)S(1)}, s32[192]{0:T(256)S(1)}, bf16[1,192,10,256]{1,3,2,0:T(8,128)(2,1)S(1)}, ...), branch_computations={%region_7.8_spmd, %region_8.11_spmd} | conditional | flops 1527307776 | bytes 24442648 | solution.py:100
  60.6 1.7 select_reduce_fusion.1
  62.4 3.7 %bitcast_add_fusion.2 = f32[1,192,10,256]{3,1,2,0:T(8,128)} fusion(f32[1,192,10,256]{3,1,2,0:T(8,128)} %get-tuple-element.138, f32[192,10,768]{2,0,1:T(8,128)S(1)} %get-tuple-element.241, f32[192,10]{0,1:T(8,128)S(1)} %get-tuple-element.239, pred[192,768]{1,0:T(8,128)(4,1)S(1)} %broadcast_compare_fusion, f32[192,10]{0,1:T(8,128)S(1)} %get-tuple-element.238, ...), kind=kOutput, calls=%fused_computation.31 | convolution fusion | flops 761856000 | bytes 10403840 | tf_op jit(solution)/shard_map/while/body/eval_jaxpr/cond/branch_1_fun/rthn,rnd->rthd/dot_general | solution.py:71
  66.1 1.7 fusion.17
  68.1 1.9 divide_convert_fusion
  70.6 1.4 copy.39
  72.8 41.4 %psum.21 = bf16[8,2560]{1,0:T(8,128)(2,1)S(1)} all-reduce(f32[8,2560]{1,0:T(8,128)S(1)} %dynamic_update_slice.3), channel_id=1, replica_groups=mesh['gx'=8,'gy'=4] {'gx','gy'}, use_global_device_ids=true, to_apply=%region_11.12 | all-reduce | flops 20480 | bytes 122880 | tf_op jit(solution)/shard_map/psum | solution.py:140
  114.5 40.6 %all-gather = bf16[32,80,8]{1,2,0:T(8,128)(2,1)S(1)} all-gather(bf16[1,80,8]{1,2,0:T(8,128)(2,1)S(1)} %fusion.37), channel_id=1, replica_groups=mesh['gx'=8,'gy'=4] {'gx','gy'}, dimensions={0}, use_global_device_ids=true | all-gather | bytes 42240 | tf_op jit(solution)/shard_map/all_gather | solution.py:145
  155.4 17.4 %fusion.56 = (f32[8]{0:T(128)S(1)}, f32[8,8000]{1,0:T(8,128)S(1)}) fusion(bf16[8000,2560]{1,0:T(8,128)(2,1)} %param.22, f32[2560,8]{0,1:T(8,128)S(1)} %reshape.940, f32[2560]{0:T(1024)S(1)} %convert_element_type.62, f32[8]{0:T(128)S(1)} %add_rsqrt_fusion), kind=kOutput, calls=%fused_computation.123 | convolution fusion | flops 327805440 | bytes 41308224 | tf_op jit(solution)/shard_map/dot_general | solution.py:151
  172.7 36.9 %pmax.7 = f32[8]{0:T(128)S(1)} all-reduce(f32[8]{0:T(128)S(1)} %get-tuple-element.250), channel_id=1, replica_groups=mesh['gx'=8,'gy'=4] {'gx','gy'}, use_global_device_ids=true, to_apply=%region_14.15 | all-reduce | flops 8 | bytes 64 | tf_op jit(solution)/shard_map/pmax | solution.py:159
  209.9 41.2 %all-reduce = (f32[8]{0:T(128)S(1)}, f32[8]{0:T(128)S(1)}) all-reduce(f32[8]{0:T(128)S(1)} %get-tuple-element.227, f32[8]{0:T(128)S(1)} %get-tuple-element.226), channel_id=1, replica_groups=mesh['gx'=8,'gy'=4] {'gx','gy'}, use_global_device_ids=true, to_apply=%region_16.17 | all-reduce | flops 16 | bytes 128 | tf_op jit(solution)/shard_map/psum | solution.py:160
  251.7 2.1 gather_fusion.2
  253.8 1.9 fusion.39
  (60 shorter events, 10.9 us)
Async XLA Ops:
  7.2 107.1 %copy-start = (bf16[2560,80]{0,1:T(8,128)(2,1)S(1)}, bf16[2560,80]{0,1:T(8,128)(2,1)}, u32[]{:S(2)}) copy-start(bf16[2560,80]{0,1:T(8,128)(2,1)} %param.19) | copy-start | bytes 1228804
  7.2 36.3 %copy-start.6 = (s32[8]{0:T(128)S(1)}, s32[8]{0:T(128)}, u32[]{:S(2)}) copy-start(s32[8]{0:T(128)} %param.23) | copy-start | bytes 100
  7.2 37.5 %all-gather.3.cloned.1.call-start = ((), (), s32[]{:S(2)}) async-start(), calls=%async_computation | async-start | bytes 2621440 | tf_op jit(solution)/shard_map/all_gather | solution.py:122
  44.7 5.7 %copy-start.2 = (bf16[1,2048,512]{2,1,0:T(8,128)(2,1)S(1)}, bf16[1,2048,512]{2,1,0:T(8,128)(2,1)}, u32[]{:S(2)}) copy-start(bf16[1,2048,512]{2,1,0:T(8,128)(2,1)} %get-tuple-element.118) | copy-start | bytes 6291460 | tf_op jit(solution)/shard_map/while/body/eval_jaxpr/cond
  68.1 46.2 %copy-start.4 = (bf16[8,80]{1,0:T(8,128)(2,1)S(1)}, bf16[8,80]{1,0:T(8,128)(2,1)}, u32[]{:S(2)}) copy-start(bf16[8,80]{1,0:T(8,128)(2,1)} %param.20) | copy-start | bytes 3844
  155.3 96.3 %copy-start.1 = (bf16[1,2048,512]{2,1,0:T(8,128)(2,1)S(1)}, bf16[1,2048,512]{2,1,0:T(8,128)(2,1)}, u32[]{:S(2)}) copy-start(bf16[1,2048,512]{2,1,0:T(8,128)(2,1)} %all-gather.3.cloned.1.call-done) | copy-start | bytes 6291460
  155.3 98.4 %copy-start.3 = (bf16[512,512]{1,0:T(8,128)(2,1)S(1)}, bf16[512,512]{1,0:T(8,128)(2,1)}, u32[]{:S(2)}) copy-start(bf16[512,512]{1,0:T(8,128)(2,1)} %gather_fusion.1) | copy-start | bytes 1572868
  209.7 42.0 %copy-start.5 = (f32[8]{0:T(128)}, f32[8]{0:T(128)S(1)}, u32[]{:S(2)}) copy-start(f32[8]{0:T(128)S(1)} %pmax.7) | copy-start | bytes 100
Sparse Core Ops, SparseCore 0:
  9.6 29.4 all-gather.2
where the time goes:
time: 263 us
  blocking collectives  175 us (67%)
  matrix products  34.1 us (13%)
  other arithmetic  23 us (9%)
  between operations  16.9 us (6%)
  local copies, waits for them, and re-layouts  12.9 us (5%)
    psum x1, blocking collectives, on_device(): last_mixed = lax.psum(padded, ('gx', 'gy')).astype(jnp.bfloat16)  41.4 us
    psum x1, blocking collectives, on_device(): lax.psum((jnp.sum(jnp.exp(logits - top_logit[:, None]), axis=1), picked),...  41.2 us
    all_gather x1, blocking collectives, on_device(): lax.all_gather(last_hidden, ('gx', 'gy'), axis=1, tiled=True)  40.6 us
    pmax x1, blocking collectives, on_device(): top_logit = lax.pmax(local_top, ('gx', 'gy'))  36.9 us
    dot_general x1, matrix products, on_device(): lax.dot_general(normed, head, (((1,), (1,)), ((), ())), preferred_element...  17.4 us
    all_gather x1, blocking collectives, on_device(): lax.all_gather(new_kv, 'gy', axis=1, tiled=True)  14.6 us
    dot_general x2, matrix products, attend(): jnp.einsum('rthn,rnd->rthd', weights.astype(jnp.bfloat16), key_rows[:, :,...  9.09 us
    dot_general x2, matrix products, attend(): jnp.einsum('rthd,rnd->rthn', query_heads, key_rows[:, :, :head_dim], pref...  7.42 us
  transfers between devices with their start and end apart: 1, of which 0 were waited for; matrix products, arithmetic and copies ran while one was open for 7% of the time, Pallas kernels for 0%

commit v1 on v0

--- a/solution.py
+++ b/solution.py
@@ -137,7 +137,7 @@
     padded = lax.dynamic_update_slice_in_dim(
         padded, last_local.astype(jnp.float32) * holder, lax.axis_index("gx") * req_local, 0
     )
-    last_mixed = lax.psum(padded, ("gx", "gy")).astype(jnp.bfloat16)
+    last_mixed = lax.all_gather(padded, axis_name=("gx", "gy")).sum(axis=0).astype(jnp.bfloat16)
     last_hidden = (
         last_residual.astype(jnp.float32)
         + jnp.dot(last_mixed, w_out, preferred_element_type=jnp.float32)

time: 263 us -> 275 us (1.046)
  waiting for transfers between devices: 0.68 us -> 52.5 us
  blocking collectives: 175 us -> 132 us
  local copies, waits for them, and re-layouts: 12.9 us -> 15.9 us
    all_gather x0 -> x1, waiting for transfers between devices: none -> 43.8 us  [on_device(): lax.all_gather(padded, axis_name=('gx', 'gy')).sum(axis=0)]
    psum x1 -> x0, blocking collectives: 41.4 us -> none  [on_device(): last_mixed = lax.psum(padded, ('gx', 'gy')).astype(jnp.bfloat16)]
    all_gather x1, waiting for transfers between devices: 0.01 us -> 7.99 us  [on_device(): lax.all_gather(cache_pool, 'gy', axis=1, tiled=True)]
  transfers between devices with their start and end apart: 1 -> 2, of which waited for: 0 -> 2; matrix products, arithmetic and copies ran while one was open for 7% -> 7% of each run, Pallas kernels for 0% -> 0%
where the time goes in v1:
time: 275 us
  blocking collectives  132 us (48%)
  waiting for transfers between devices  52.5 us (19%)
  matrix products  34.3 us (12%)
  other arithmetic  23.4 us (9%)
  between operations  16.9 us (6%)
  local copies, waits for them, and re-layouts  15.9 us (6%)
    all_gather x1, waiting for transfers between devices, on_device(): lax.all_gather(padded, axis_name=('gx', 'gy')).sum(axis=0)  43.8 us
    psum x1, blocking collectives, on_device(): lax.psum((jnp.sum(jnp.exp(logits - top_logit[:, None]), axis=1), picked),...  41.2 us
    all_gather x1, blocking collectives, on_device(): lax.all_gather(last_hidden, ('gx', 'gy'), axis=1, tiled=True)  39.6 us
    pmax x1, blocking collectives, on_device(): top_logit = lax.pmax(local_top, ('gx', 'gy'))  36.9 us
    dot_general x1, matrix products, on_device(): lax.dot_general(normed, head, (((1,), (1,)), ((), ())), preferred_element...  17.2 us
    all_gather x1, blocking collectives, on_device(): lax.all_gather(new_kv, 'gy', axis=1, tiled=True)  13.9 us
    dot_general x2, matrix products, attend(): jnp.einsum('rthn,rnd->rthd', weights.astype(jnp.bfloat16), key_rows[:, :,...  9.13 us
    all_gather x1, waiting for transfers between devices, on_device(): lax.all_gather(cache_pool, 'gy', axis=1, tiled=True)  7.99 us
  transfers between devices with their start and end apart: 2, of which 2 were waited for; matrix products, arithmetic and copies ran while one was open for 7% of the time, Pallas kernels for 0%

profile of v1, /device:TPU:0, one launch (start us, length us, event | category | flops | bytes accessed | tf_op | source)
XLA Modules:
  0.0 274.8 jit_solution(1033040199129981914)
XLA Ops:
  16.5 13.9 %all_gather.14 = bf16[1,768,512]{2,1,0:T(8,128)(2,1)S(1)} all-gather(bf16[1,192,512]{2,1,0:T(8,128)(2,1)S(1)} %copy-done.4), channel_id=1, replica_groups=mesh['gx'=8,'gy'=4] {'gy'}, dimensions={1}, use_global_device_ids=true | all-gather | bytes 983040 | tf_op jit(solution)/shard_map/all_gather | solution.py:125
  30.5 8.0 %all-gather.4.cloned.1.call-done = bf16[1,2048,512]{2,1,0:T(8,128)(2,1)} async-done(((bf16[1,512,512]{2,1,0:T(8,128)(2,1)}), bf16[1,2048,512]{2,1,0:T(8,128)(2,1)}) %all-gather.4.cloned.1.call-update) | async-done | bytes 2097168 | tf_op jit(solution)/shard_map/all_gather | solution.py:122
  38.5 15.9 %conditional.2 = ((f32[1,192,10]{1,2,0:T(8,128)S(1)}, f32[1,192,10]{1,2,0:T(8,128)S(1)}, f32[1,192,10,256]{3,1,2,0:T(8,128)})) conditional(s32[]{:T(128)} %convert_element_type.48, (f32[1,192,10]{1,2,0:T(8,128)S(1)}, f32[1,192,10]{1,2,0:T(8,128)S(1)}, f32[1,192,10,256]{3,1,2,0:T(8,128)}) %tuple.31, (pred[1,192,2048]{2,1,0:T(8,128)(4,1)S(1)}, ...), branch_computations={%region_3.4_spmd, %region_4.7_spmd} | conditional | flops 4070774272 | bytes 63906876 | solution.py:100
  38.5 5.8 %select_reduce_fusion = (f32[192,10]{0,1:T(8,128)S(1)}, f32[192,10,2048]{2,0,1:T(8,128)S(1)}) fusion(pred[192,2048]{1,0:T(8,128)(4,1)S(1)} %bitcast.102, bf16[1,2048,512]{2,1,0:T(8,128)(2,1)} %get-tuple-element.118, bf16[1,192,10,256]{1,3,2,0:T(8,128)(2,1)S(1)} %get-tuple-element.209), kind=kOutput, calls=%fused_computation.4 | convolution fusion | flops 2025060480 | bytes 18161152 | tf_op jit(solution)/shard_map/while/body/eval_jaxpr/cond/branch_1_fun/rthd,rnd->rthn/dot_general | solution.py:57
  44.3 5.4 %bitcast_add_fusion = f32[1,192,10,256]{3,1,2,0:T(8,128)} fusion(f32[1,192,10,256]{3,1,2,0:T(8,128)} %get-tuple-element.120, f32[192,10,2048]{2,0,1:T(8,128)S(1)} %get-tuple-element.243, f32[192,10]{0,1:T(8,128)S(1)} %bitcast.108, pred[192,2048]{1,0:T(8,128)(4,1)S(1)} %bitcast.103, bf16[1,2048,512]{2,1,0:T(8,128)(2,1)S(1)} %copy-done.2, ...), kind=kOutput, calls=%fused_computation.9 | convolution fusion | flops 2029977600 | bytes 21135360 | tf_op jit(solution)/shard_map/while/body/eval_jaxpr/cond/branch_1_fun/rthn,rnd->rthd/dot_general | solution.py:71
  49.7 4.7 %fusion.1 = f32[192,10]{0,1:T(8,128)S(1)} fusion(f32[192,10,2048]{2,0,1:T(8,128)S(1)} %get-tuple-element.243, f32[192,10]{0,1:T(8,128)S(1)} %bitcast.109, pred[192,2048]{1,0:T(8,128)(4,1)S(1)} %bitcast.104), kind=kLoop, calls=%fused_computation.6 | loop fusion | flops 15726720 | bytes 16137216 | tf_op jit(solution)/shard_map/while/body/eval_jaxpr/cond/branch_1_fun/reduce_sum | solution.py:70
  54.4 7.5 %conditional.3 = ((f32[1,192,10]{1,2,0:T(8,128)S(1)}, f32[1,192,10,256]{3,1,2,0:T(8,128)})) conditional(s32[]{:T(128)} %convert_element_type.47, (f32[1,192,10]{1,2,0:T(8,128)S(1)}, f32[1,192,10,256]{3,1,2,0:T(8,128)}) %tuple.33, (s32[768]{0:T(1024)S(1)}, s32[192]{0:T(256)S(1)}, bf16[1,192,10,256]{1,3,2,0:T(8,128)(2,1)S(1)}, ...), branch_computations={%region_7.8_spmd, %region_8.11_spmd} | conditional | flops 1527307776 | bytes 24442648 | solution.py:100
  54.6 1.8 select_reduce_fusion.1
  56.4 3.8 %bitcast_add_fusion.2 = f32[1,192,10,256]{3,1,2,0:T(8,128)} fusion(f32[1,192,10,256]{3,1,2,0:T(8,128)} %get-tuple-element.138, f32[192,10,768]{2,0,1:T(8,128)S(1)} %get-tuple-element.241, f32[192,10]{0,1:T(8,128)S(1)} %get-tuple-element.239, pred[192,768]{1,0:T(8,128)(4,1)S(1)} %broadcast_compare_fusion, f32[192,10]{0,1:T(8,128)S(1)} %get-tuple-element.238, ...), kind=kOutput, calls=%fused_computation.31 | convolution fusion | flops 761856000 | bytes 10403840 | tf_op jit(solution)/shard_map/while/body/eval_jaxpr/cond/branch_1_fun/rthn,rnd->rthd/dot_general | solution.py:71
  60.2 1.7 fusion.17
  62.0 3.0 %divide_convert_fusion = bf16[1,192,10,256]{3,1,2,0:T(8,128)(2,1)} fusion(f32[1,192,10,256]{3,1,2,0:T(8,128)} %get-tuple-element.152, f32[192,10]{0,1:T(8,128)S(1)} %bitcast.107), kind=kLoop, calls=%fused_computation.46 | loop fusion | flops 983040 | bytes 2956800 | tf_op jit(solution)/shard_map/convert_element_type | solution.py:130
  64.9 2.4 copy.43
  67.3 2.3 copy.47
  73.4 2.6 compare_select_fusion
  76.1 2.6 gather_fusion.1
  78.7 2.6 compare_select_fusion.3
  81.4 2.0 gather_fusion.2
  83.3 2.2 fusion.40
  85.6 43.8 %all-gather.6.cloned.1.call-done = f32[32,8,2560]{2,1,0:T(8,128)} async-done(((f32[1,8,2560]{2,1,0:T(8,128)}), f32[32,8,2560]{2,1,0:T(8,128)}) %all-gather.6.cloned.1.call-update) | async-done | bytes 2621456 | tf_op jit(solution)/shard_map/all_gather | solution.py:140
  129.4 1.9 reduce_sum.71
  131.9 39.6 %all-gather = bf16[32,80,8]{1,2,0:T(8,128)(2,1)S(1)} all-gather(bf16[1,80,8]{1,2,0:T(8,128)(2,1)S(1)} %fusion.37), channel_id=1, replica_groups=mesh['gx'=8,'gy'=4] {'gx','gy'}, dimensions={0}, use_global_device_ids=true | all-gather | bytes 42240 | tf_op jit(solution)/shard_map/all_gather | solution.py:145
  171.8 17.2 %fusion.57 = (f32[8]{0:T(128)S(1)}, f32[8,8000]{1,0:T(8,128)S(1)}) fusion(bf16[8000,2560]{1,0:T(8,128)(2,1)} %param.22, f32[2560,8]{0,1:T(8,128)S(1)} %reshape.927, f32[2560]{0:T(1024)S(1)} %convert_element_type.56, f32[8]{0:T(128)S(1)} %add_rsqrt_fusion), kind=kOutput, calls=%fused_computation.124 | convolution fusion | flops 327805440 | bytes 41308224 | tf_op jit(solution)/shard_map/dot_general | solution.py:151
  189.0 36.9 %pmax.7 = f32[8]{0:T(128)S(1)} all-reduce(f32[8]{0:T(128)S(1)} %get-tuple-element.250), channel_id=1, replica_groups=mesh['gx'=8,'gy'=4] {'gx','gy'}, use_global_device_ids=true, to_apply=%region_14.15 | all-reduce | flops 8 | bytes 64 | tf_op jit(solution)/shard_map/pmax | solution.py:159
  226.2 41.2 %all-reduce = (f32[8]{0:T(128)S(1)}, f32[8]{0:T(128)S(1)}) all-reduce(f32[8]{0:T(128)S(1)} %get-tuple-element.227, f32[8]{0:T(128)S(1)} %get-tuple-element.226), channel_id=1, replica_groups=mesh['gx'=8,'gy'=4] {'gx','gy'}, use_global_device_ids=true, to_apply=%region_16.17 | all-reduce | flops 16 | bytes 128 | tf_op jit(solution)/shard_map/psum | solution.py:160
  (69 shorter events, 12.4 us)
Async XLA Ops:
  7.2 124.4 %copy-start = (bf16[2560,80]{0,1:T(8,128)(2,1)S(1)}, bf16[2560,80]{0,1:T(8,128)(2,1)}, u32[]{:S(2)}) copy-start(bf16[2560,80]{0,1:T(8,128)(2,1)} %param.19) | copy-start | bytes 1228804
  7.2 9.4 %copy-start.4 = (bf16[1,192,512]{2,1,0:T(8,128)(2,1)S(1)}, bf16[1,192,512]{2,1,0:T(8,128)(2,1)}, u32[]{:S(2)}) copy-start(bf16[1,192,512]{2,1,0:T(8,128)(2,1)} %param.15) | copy-start | bytes 589828
  7.2 31.3 %all-gather.4.cloned.1.call-start = ((), (), s32[]{:S(2)}) async-start(), calls=%async_computation | async-start | bytes 2621440 | tf_op jit(solution)/shard_map/all_gather | solution.py:122
  7.9 121.4 %all-gather.6.cloned.1.call-start = ((), (), s32[]{:S(2)}) async-start(), calls=%async_computation.1 | async-start | bytes 2703360 | tf_op jit(solution)/shard_map/all_gather | solution.py:140
  38.5 5.9 %copy-start.2 = (bf16[1,2048,512]{2,1,0:T(8,128)(2,1)S(1)}, bf16[1,2048,512]{2,1,0:T(8,128)(2,1)}, u32[]{:S(2)}) copy-start(bf16[1,2048,512]{2,1,0:T(8,128)(2,1)} %get-tuple-element.118) | copy-start | bytes 6291460 | tf_op jit(solution)/shard_map/while/body/eval_jaxpr/cond
  61.9 9.6 %copy-start.6 = (bf16[2560]{0:T(1024)(128)(2,1)S(1)}, bf16[2560]{0:T(1024)(128)(2,1)}, u32[]{:S(2)}) copy-start(bf16[2560]{0:T(1024)(128)(2,1)} %param.21) | copy-start | bytes 15364
  61.9 10.9 %copy-start.5 = (s32[1,4]{1,0:T(1,128)S(1)}, s32[1,4]{1,0:T(1,128)}, u32[]{:S(2)}) copy-start(s32[1,4]{1,0:T(1,128)} %param.18) | copy-start | bytes 52
  62.0 19.3 %copy-start.9 = (s32[8]{0:T(128)S(1)}, s32[8]{0:T(128)}, u32[]{:S(2)}) copy-start(s32[8]{0:T(128)} %param.23) | copy-start | bytes 100
  62.0 19.4 %copy-start.1 = (bf16[1,2048,512]{2,1,0:T(8,128)(2,1)S(1)}, bf16[1,2048,512]{2,1,0:T(8,128)(2,1)}, u32[]{:S(2)}) copy-start(bf16[1,2048,512]{2,1,0:T(8,128)(2,1)} %all-gather.4.cloned.1.call-done) | copy-start | bytes 6291460
  70.9 0.6 copy-start.3
  78.7 52.9 %copy-start.7 = (bf16[8,80]{1,0:T(8,128)(2,1)S(1)}, bf16[8,80]{1,0:T(8,128)(2,1)}, u32[]{:S(2)}) copy-start(bf16[8,80]{1,0:T(8,128)(2,1)} %param.20) | copy-start | bytes 3844
  225.9 42.0 %copy-start.8 = (f32[8]{0:T(128)}, f32[8]{0:T(128)S(1)}, u32[]{:S(2)}) copy-start(f32[8]{0:T(128)S(1)} %pmax.7) | copy-start | bytes 100
Sparse Core Ops, SparseCore 0:
  9.6 28.8 all-gather.3
  71.7 57.6 all-gather.5
